TPU v7x, 32 devices: a whole 2x2x4 slice. The times are simulated.
32 devices in a mesh: groups: 2 (over y), seq: 4 (over z), chan: 2 (over x), pair: 2 (over core).
Axes of the slice: x: 2, y: 2, z: 4, core: 2. Of those that a mesh axis runs over, the one named last changes fastest.
Arguments:
- tokens: int32 [1024], P(('groups', 'seq')), parts along dimension 0, may hold values from 0 to 4
- kmer_table: bfloat16 [4, 5, 2048], replicated, may hold values from -3 to 3
- norm_gain: float32 [2048], replicated, may hold values from 0.3 to 2, as said below
- in_proj: bfloat16 [2048, 3, 2048], P(None, None, ('chan', 'pair')), may hold values from -0.125 to 0.125
- long_filter: float32 [4, 4, 128, 512], P(('chan', 'pair'), 'seq'), may hold values from -1 to 1, as said below
- out_proj: bfloat16 [2048, 2048], P(None, ('chan', 'pair')), may hold values from -0.125 to 0.125
- cotangent: bfloat16 [1024, 2048], P(('groups', 'seq'), ('chan', 'pair')), parts along dimension 0, may hold values from -6 to 6
Outputs:
- block_out: bfloat16 [1024, 2048], P(('groups', 'seq'), ('chan', 'pair')), parts along dimension 0
- filter_grad: float32 [8, 4, 128, 512], P(('groups', 'chan', 'pair'), 'seq'), parts along dimension 0
- kmer_grad: float32 [8, 5, 2048], P('groups', None, ('chan', 'pair')), parts along dimension 0
- gain_grad: float32 [4096], P(('groups', 'chan', 'pair')), parts along dimension 0
There are 2 independent parts, one for each index of `groups`. A program takes and returns all parts, laid end to end along the dimension named above; an argument that names none is the same for every part. Nothing has to cross between parts.
Inputs may be any that keep to these rules, and one draw needn't show every extreme that they name: `tokens`: nucleotide ids: 0 to 3 for A, C, G, T and 4 for N. `long_filter`: a causal filter for each channel. `norm_gain`: a positive gain for each channel.
All inputs are finite; a program needn't handle non-finite values.
Results may differ from a plain program's by a relative error of at most 0.0072.
Values may be sent and summed in bfloat16 or wider, within the bound.
No kernel may reach another device: no remote copies, remote signals or barrier semaphores. Data moves between devices by JAX's collectives and lax.ppermute only.
A program may use at most 128 MiB of HBM per device.

v0:
```python
import math
import jax
import jax.numpy as jnp
from jax import lax
from jax.sharding import PartitionSpec as P

NORM_EPSILON = 1e-05
PRECISE = lax.Precision.HIGHEST
TRANSFORM_PRECISION = lax.Precision.HIGH


def from_behind(value, axis, steps):
    count = lax.axis_size(axis)
    first, last = (max(0, -steps), min(count, count - steps))
    return lax.ppermute(value, axis, [(source, source + steps) for source in range(first, last)])


def dft_matrix(length):
    total = 2 * length
    t = lax.optimization_barrier(lax.broadcasted_iota(jnp.int32, (length, 1), 0))
    j = lax.broadcasted_iota(jnp.int32, (1, total), 1)
    k = jnp.where(j < length, j, j - length)
    k = jnp.where(j == length, length, k)
    idx = t * k % total
    idx = jnp.where(j > length, (idx + 3 * total // 4) % total, idx)
    idx = jnp.where(idx >= length, idx - total, idx)
    return lax.optimization_barrier(jnp.cos(idx.astype(jnp.float32) * (2.0 * math.pi / total)))


def forward_dft(signal, dft):
    return jnp.dot(signal.astype(jnp.float32), dft, precision=TRANSFORM_PRECISION)


def inverse_dft(spec, dft):
    length = dft.shape[0]
    total = 2 * length
    col = lax.broadcasted_iota(jnp.int32, (1, total), 1)
    weight = jnp.where(col % length == 0, 1.0 / total, 2.0 / total).astype(jnp.float32)
    return lax.dot_general(
        spec * weight, dft, (((1,), (1,)), ((), ())), precision=TRANSFORM_PRECISION
    )


def halves(spec):
    length = spec.shape[1] // 2
    return (spec[:, :length], spec[:, length:])


def first_col(shape):
    return lax.broadcasted_iota(jnp.int32, shape, 1) == 0


def cmul(ga, gb, xa, xb, conj_g):
    edge = first_col(ga.shape)
    sign = -1.0 if conj_g else 1.0
    ya = ga * xa - sign * (gb * xb)
    yb = ga * xb + sign * (gb * xa)
    ya = jnp.where(edge, ga * xa, ya)
    yb = jnp.where(edge, gb * xb, yb)
    return jnp.concatenate([ya, yb], axis=1)


def pair_flip(values):
    rows = lax.broadcasted_iota(jnp.int32, values.shape, 0)
    up = jnp.roll(values, -1, axis=0)
    down = jnp.roll(values, 1, axis=0)
    return jnp.where(rows % 2 == 0, up, down)


def add_conj_flip(spec):
    a, b = halves(spec)
    fa, fb = halves(pair_flip(spec))
    edge = first_col(a.shape)
    return jnp.concatenate([a + fa, jnp.where(edge, b + fb, b - fb)], axis=1)


def per_device(tokens, kmer_table, norm_gain, in_proj, long_filter, out_proj, cotangent):
    row_count = tokens.shape[0]
    kmer_len, letter_count, model_width = kmer_table.shape
    local_width = in_proj.shape[2]
    length = row_count * lax.axis_size("seq")
    group_index = lax.axis_index(("chan", "pair"))
    rim_width = kmer_len - 1
    before = from_behind(tokens[row_count - rim_width :] + 1, "seq", 1) - 1
    extended = jnp.concatenate([before, tokens])
    letters = jnp.arange(letter_count, dtype=jnp.int32)
    columns = []
    for shift_back in range(kmer_len):
        window = extended[rim_width - shift_back : rim_width - shift_back + row_count]
        columns.append(window[:, None] == letters[None, :])
    onehot_t = jnp.concatenate(columns, axis=1).T.astype(jnp.bfloat16)
    table_t = kmer_table.reshape(kmer_len * letter_count, model_width).T
    embedded = jnp.dot(table_t, onehot_t, preferred_element_type=jnp.float32)
    inv_rms = lax.rsqrt(jnp.mean(embedded * embedded, axis=0, keepdims=True) + NORM_EPSILON)
    normed = embedded * inv_rms
    hidden = (normed * norm_gain[:, None]).astype(jnp.bfloat16)
    projected = jnp.einsum("dr,dmc->mcr", hidden, in_proj, preferred_element_type=jnp.float32)
    query_part = projected[0]
    key_part = projected[1]
    value_part = projected[2]
    mixed_in = (key_part * value_part).astype(jnp.bfloat16)
    dft = dft_matrix(length)
    filter_rows = long_filter.reshape(long_filter.shape[2], long_filter.shape[3])
    spec_g = add_conj_flip(forward_dft(filter_rows, dft))
    ga, gb = halves(spec_g)
    mixed_cols = lax.all_to_all(mixed_in, "seq", split_axis=0, concat_axis=1, tiled=True)
    spec_s = forward_dft(mixed_cols, dft)
    sa, sb = halves(spec_s)
    conv_cols = inverse_dft(cmul(ga, gb, sa, sb, False), dft).astype(jnp.bfloat16)
    conv_rows = lax.all_to_all(conv_cols, "seq", split_axis=1, concat_axis=0, tiled=True)
    gated_rows = (query_part * conv_rows.astype(jnp.float32)).astype(jnp.bfloat16)
    weight_rows = out_proj
    mixed_out = jnp.einsum(
        "cr,cd->rd",
        lax.all_gather(gated_rows, ("chan", "pair"), axis=0, tiled=True),
        weight_rows,
        preferred_element_type=jnp.float32,
    )
    own_rows = lax.dynamic_slice_in_dim(embedded, group_index * local_width, local_width, 0)
    block_out = (mixed_out + own_rows.T).astype(jnp.bfloat16)
    grad_scale = 1.0 / math.sqrt(length)
    d_gated = (
        lax.psum_scatter(
            jnp.einsum("cd,rd->cr", weight_rows, cotangent, preferred_element_type=jnp.float32),
            ("chan", "pair"),
            scatter_dimension=0,
            tiled=True,
        )
        * grad_scale
    )
    d_conv = (d_gated * query_part).astype(jnp.bfloat16)
    d_query = d_gated * conv_rows.astype(jnp.float32)
    d_cols = lax.all_to_all(d_conv, "seq", split_axis=0, concat_axis=1, tiled=True)
    spec_d = forward_dft(d_cols, dft)
    da, db = halves(spec_d)
    d_mixed_cols = inverse_dft(cmul(ga, gb, da, db, True), dft).astype(jnp.bfloat16)
    d_mixed = lax.all_to_all(d_mixed_cols, "seq", split_axis=1, concat_axis=0, tiled=True)
    cross = cmul(sa, sb, da, db, True)
    filter_grad = inverse_dft(add_conj_flip(cross), dft)
    d_key = d_mixed.astype(jnp.float32) * value_part
    d_value = d_mixed.astype(jnp.float32) * key_part
    d_proj = jnp.stack([d_query, d_key, d_value]).astype(jnp.bfloat16)
    normed_local = lax.dynamic_slice_in_dim(normed, group_index * local_width, local_width, 0)
    cot_scaled = cotangent.T.astype(jnp.float32) * grad_scale
    d_full = lax.psum(
        jnp.einsum("dmc,mcr->dr", in_proj, d_proj, preferred_element_type=jnp.float32),
        ("chan", "pair"),
    )
    scaled_full = norm_gain[:, None] * d_full
    row_stat = jnp.mean(scaled_full * normed, axis=0, keepdims=True)
    scaled = lax.dynamic_slice_in_dim(scaled_full, group_index * local_width, local_width, 0)
    d_embedded = inv_rms * (scaled - normed_local * row_stat) + cot_scaled
    d_hidden = lax.dynamic_slice_in_dim(d_full, group_index * local_width, local_width, 0)
    gain_part = jnp.sum(d_hidden * normed_local, axis=1)
    table_part = jnp.einsum(
        "kr,cr->kc", onehot_t.astype(jnp.float32), d_embedded, precision=PRECISE
    )
    summed = lax.psum(jnp.concatenate([table_part, gain_part[None, :]], axis=0), "seq")
    kmer_grad = summed[: kmer_len * letter_count]
    gain_grad = summed[kmer_len * letter_count]
    return (
        block_out,
        filter_grad.reshape(long_filter.shape),
        kmer_grad.reshape(kmer_len, letter_count, local_width),
        gain_grad,
    )


def solution(mesh):
    in_specs = (
        P(("groups", "seq")),
        P(),
        P(),
        P(None, None, ("chan", "pair")),
        P(("chan", "pair"), "seq", None, None),
        P(None, ("chan", "pair")),
        P(("groups", "seq"), ("chan", "pair")),
    )
    out_specs = (
        P(("groups", "seq"), ("chan", "pair")),
        P(("groups", "chan", "pair"), "seq", None, None),
        P("groups", None, ("chan", "pair")),
        P(("groups", "chan", "pair")),
    )
    return jax.shard_map(
        per_device, mesh=mesh, in_specs=in_specs, out_specs=out_specs, check_vma=False
    )
```

profile of v0, /device:TPU:0, one launch (start us, length us, event | category | flops | bytes accessed | tf_op | source)
XLA Modules:
  0.0 173.6 jit_solution(6065162141426624654)
XLA Ops:
  8.1 5.1 %collective-permute-start = (s32[3]{0:T(128)S(1)}, s32[3]{0:T(128)S(1)}, u32[]{:S(2)}, u32[]{:S(2)}) collective-permute-start(s32[3]{0:T(128)S(1)} %slice_add_fusion.2), channel_id=1, source_target_pairs={{0,4},{4,8},{8,12},{1,5},{5,9},{9,13},{2,6},{6,10},{10,14},{3,7},{... | collective-permute-start | bytes 44 | tf_op jit(solution)/shard_map/ppermute | solution.py:15
  13.2 2.7 %fusion.66 = f32[2048,128]{0,1:T(8,128)} fusion(bf16[2048,512]{1,0:T(8,128)(2,1)S(1)} %copy-done, bf16[128,512]{1,0:T(8,128)(2,1)} %param.13), kind=kOutput, calls=%fused_computation.144 | convolution fusion | flops 268435456 | bytes 3276800 | tf_op jit(solution)/shard_map/cd,rd->cr/dot_general | solution.py:124
  16.0 8.7 %fusion.5 = f32[512,1024]{1,0:T(8,128)S(1)} fusion(s32[1024]{0:T(1024)S(1)} %fusion.50, s32[512]{0:T(512)S(1)} %bitcast.109, pred[1024]{0:T(1024)(128)(4,1)S(1)} %iota_compare_fusion.1), kind=kLoop, calls=%fused_computation.15 | loop fusion | flops 15728640 | bytes 2104320 | tf_op jit(solution)/shard_map/cos | solution.py:27
  28.7 4.7 %convolution_bitcast_fusion.1 = f32[3,512,128]{1,2,0:T(8,128)} fusion(bf16[2048,3,512]{2,0,1:T(8,128)(2,1)} %param.10, f32[128,2048]{1,0:T(8,128)S(1)} %broadcast_multiply_fusion.1, f32[2048]{0:T(1024)S(1)} %copy-done.19), kind=kOutput, calls=%fused_computation.17 | convolution fusion | flops 805830656 | bytes 8134656 | tf_op jit(solution)/shard_map/dr,dmc->mcr/dot_general | solution.py:97
  33.4 7.7 %reduce-scatter.2.cloned.1.call-done = f32[512,128]{0,1:T(8,128)} async-done(((f32[2048,128]{0,1:T(8,128)}), f32[512,128]{0,1:T(8,128)}) %reduce-scatter.2.cloned.1.call-update) | async-done | bytes 262160 | tf_op jit(solution)/shard_map/reduce_scatter | solution.py:123
  42.8 4.6 %all-to-all-start.2 = ((bf16[4,128,128]{1,2,0:T(8,128)(2,1)}), bf16[4,128,128]{1,2,0:T(8,128)(2,1)S(1)}, u32[]{:S(2)}, u32[]{:S(2)}) async-start(bf16[4,128,128]{1,2,0:T(8,128)(2,1)} %copy_bitcast_fusion), calls=%async_computation.3 | async-start | bytes 262144 | tf_op jit(solution)/shard_map/all_to_all | solution.py:133
  47.4 2.1 %maximum_select_fusion = f32[128,1024]{1,0:T(8,128)} fusion(f32[1,1024]{1,0:T(1,128)S(1)} %get-tuple-element.35, f32[127,1024]{1,0:T(8,128)} %get-tuple-element.37, f32[127,1024]{1,0:T(8,128)} %get-tuple-element.36, f32[1,1024]{1,0:T(1,128)S(1)} %get-tuple-element.34, s32[128]{0:T(128)S(1)} %iota_and_fusion.1, s32[128]{0:T(128)S(1)} %broadcast_add_fusion, ...), kind=kLoop, calls=%fused_computation.40 | loop fusion | flops 655360 | bytes 1574016 | tf_op jit(solution)/shard_map/jit(_where)/select_n | solution.py:67
  49.5 3.9 %all-to-all-done.2 = bf16[4,128,128]{1,2,0:T(8,128)(2,1)S(1)} async-done(((bf16[4,128,128]{1,2,0:T(8,128)(2,1)}), bf16[4,128,128]{1,2,0:T(8,128)(2,1)S(1)}, u32[]{:S(2)}, u32[]{:S(2)}) %all-to-all-start.2) | async-done | bytes 131104 | tf_op jit(solution)/shard_map/all_to_all | solution.py:133
  53.5 2.2 %fusion.67 = f32[128,1024]{1,0:T(8,128)S(1)} fusion(bf16[128,512]{0,1:T(8,128)(2,1)S(1)} %bitcast.106, f32[512,1024]{1,0:T(8,128)} %copy-done.1), kind=kOutput, calls=%fused_computation.145 | convolution fusion | flops 402653184 | bytes 2752512 | tf_op jit(solution)/shard_map/dot_general | solution.py:31
  59.0 8.3 %all_to_all.61 = bf16[128,4,128]{0,2,1:T(8,128)(2,1)S(1)} all-to-all(bf16[128,4,128]{0,2,1:T(8,128)(2,1)S(1)} %bitcast.104), channel_id=1, replica_groups=mesh['groups'=2,'seq'=4,'chan'=2,'pair'=2] {'seq'}, dimensions={1} | all-to-all | bytes 262144 | tf_op jit(solution)/shard_map/all_to_all | solution.py:137
  68.3 1.8 %multiply_convert_fusion.1 = (bf16[1,512,128]{1,2,0:T(8,128)(2,1)S(1)}, bf16[1,512,128]{1,2,0:T(8,128)(2,1)}, bf16[1,512,128]{1,2,0:T(8,128)(2,1)S(1)}) fusion(f32[1,512,128]{1,2,0:T(8,128)} %reshape.116, f32[3,512,128]{1,2,0:T(8,128)} %convolution_bitcast_fusion.1), kind=kLoop, calls=%fused_computation.83 | loop fusion | flops 393216 | bytes 1179648 | tf_op jit(solution)/shard_map/convert.5
  70.9 3.3 %all-to-all-start = ((bf16[4,128,128]{1,2,0:T(8,128)(2,1)}), bf16[4,128,128]{1,2,0:T(8,128)(2,1)S(1)}, u32[]{:S(2)}, u32[]{:S(2)}) async-start(bf16[4,128,128]{1,2,0:T(8,128)(2,1)} %copy.23), calls=%async_computation | async-start | bytes 262144 | tf_op jit(solution)/shard_map/all_to_all | solution.py:106
  74.2 5.9 %all-to-all-done = bf16[4,128,128]{1,2,0:T(8,128)(2,1)S(1)} async-done(((bf16[4,128,128]{1,2,0:T(8,128)(2,1)}), bf16[4,128,128]{1,2,0:T(8,128)(2,1)S(1)}, u32[]{:S(2)}, u32[]{:S(2)}) %all-to-all-start) | async-done | bytes 131104 | tf_op jit(solution)/shard_map/all_to_all | solution.py:106
  80.1 2.2 %fusion.65 = f32[128,1024]{1,0:T(8,128)S(1)} fusion(bf16[128,512]{0,1:T(8,128)(2,1)S(1)} %bitcast.105, f32[512,1024]{1,0:T(8,128)} %copy-done.1), kind=kOutput, calls=%fused_computation.143 | convolution fusion | flops 402653184 | bytes 2752512 | tf_op jit(solution)/shard_map/dot_general | solution.py:31
  85.2 1.8 %convolution_convert_fusion.1 = bf16[128,512]{1,0:T(8,128)(2,1)} fusion(f32[512,1024]{1,0:T(8,128)S(1)} %copy-done.3, f32[128,512]{1,0:T(8,128)S(1)} %get-tuple-element.28, f32[128,512]{1,0:T(8,128)S(1)} %get-tuple-element.29, f32[1024]{0:T(1024)S(1)} %fusion.54), kind=kOutput, calls=%fused_computation.23 | convolution fusion | flops 402980864 | bytes 2756608 | tf_op jit(solution)/shard_map/dot_general | solution.py:39
  88.8 4.0 %all-to-all-start.1 = ((bf16[128,4,128]{0,2,1:T(8,128)(2,1)}), bf16[128,4,128]{0,2,1:T(8,128)(2,1)}, u32[]{:S(2)}, u32[]{:S(2)}) async-start(bf16[128,4,128]{0,2,1:T(8,128)(2,1)} %bitcast.103), calls=%async_computation.1 | async-start | bytes 262144 | tf_op jit(solution)/shard_map/all_to_all | solution.py:110
  94.1 1.9 %slice_add_fusion = (f32[128,512]{1,0:T(8,128)}, f32[128,512]{1,0:T(8,128)}) fusion(f32[128,512]{1,0:T(8,128)S(1)} %get-tuple-element.21, f32[128,1024]{1,0:T(8,128)S(1)} %fusion.14, f32[128,512]{1,0:T(8,128)} %copy-done.10, pred[512]{0:T(512)(128)(4,1)} %copy-done.24), kind=kLoop, calls=%fused_computation.66 | loop fusion | flops 262144 | bytes 1573376 | tf_op jit(solution)/shard_map/add | solution.py:74
  95.9 2.8 %all-to-all-done.1 = bf16[128,4,128]{0,2,1:T(8,128)(2,1)} async-done(((bf16[128,4,128]{0,2,1:T(8,128)(2,1)}), bf16[128,4,128]{0,2,1:T(8,128)(2,1)}, u32[]{:S(2)}, u32[]{:S(2)}) %all-to-all-start.1) | async-done | bytes 131104 | tf_op jit(solution)/shard_map/all_to_all | solution.py:110
  98.7 1.8 %fusion.43 = (bf16[1,512,128]{1,2,0:T(8,128)(2,1)S(1)}, bf16[512,128]{0,1:T(8,128)(2,1)}) fusion(f32[512,128]{0,1:T(8,128)} %reduce-scatter.2.cloned.1.call-done, f32[3,512,128]{1,2,0:T(8,128)} %convolution_bitcast_fusion.1, bf16[128,4,128]{0,2,1:T(8,128)(2,1)} %all-to-all-done.1), kind=kLoop, calls=%fused_computation.99 | loop fusion | flops 393216 | bytes 917504 | tf_op jit(solution)/shard_map/stack | solution.py:142
  100.5 6.1 %convolution_bitcast_fusion = f32[2048,128]{0,1:T(8,128)} fusion(bf16[2048,3,512]{2,0,1:T(8,128)(2,1)} %param.10, bf16[1,512,128]{1,2,0:T(8,128)(2,1)} %get-tuple-element.26, bf16[1,512,128]{1,2,0:T(8,128)(2,1)S(1)} %get-tuple-element.25, bf16[1,512,128]{1,2,0:T(8,128)(2,1)S(1)} %get-tuple-element.38), kind=kOutput, calls=%fused_computation.9 | convolution fusion | flops 805699584 | bytes 7733248 | tf_op jit(solution)/shard_map/dmc,mcr->dr/dot_general | solution.py:146
  106.6 3.6 %convolution_bitcast_fusion.3 = f32[1,1,128,512]{3,2,1,0:T(8,128)} fusion(f32[512,1024]{1,0:T(8,128)} %copy-done.1, f32[128,512]{1,0:T(8,128)} %get-tuple-element.31, f32[128,512]{1,0:T(8,128)S(1)} %copy-done.14, f32[1024]{0:T(1024)S(1)} %fusion.54), kind=kOutput, calls=%fused_computation.19 | convolution fusion | flops 402915328 | bytes 2887680 | tf_op jit(solution)/shard_map/dot_general | solution.py:39
  110.2 10.1 %all_gather.3 = bf16[2048,128]{0,1:T(8,128)(2,1)S(1)} all-gather(bf16[512,128]{0,1:T(8,128)(2,1)S(1)} %copy-done.16), channel_id=1, replica_groups=mesh['groups'=2,'seq'=4,'chan'=2,'pair'=2] {'chan','pair'}, dimensions={0}, use_global_device_ids=true | all-gather | bytes 655360 | tf_op jit(solution)/shard_map/all_gather | solution.py:115
  121.4 21.7 %all-reduce.2.cloned.1.call-done = f32[2048,128]{0,1:T(8,128)} async-done(((f32[2048,128]{0,1:T(8,128)}), f32[2048,128]{0,1:T(8,128)}) %all-reduce.2.cloned.1.call-update) | async-done | bytes 1048592 | tf_op jit(solution)/shard_map/psum | solution.py:145
  146.1 19.4 %psum.15 = f32[21,512]{1,0:T(8,128)S(1)} all-reduce(f32[21,512]{1,0:T(8,128)S(1)} %pad_maximum_fusion.1), channel_id=1, replica_groups=mesh['groups'=2,'seq'=4,'chan'=2,'pair'=2] {'seq'}, use_global_device_ids=true, to_apply=%region_5.6 | all-reduce | flops 10752 | bytes 86016 | tf_op jit(solution)/shard_map/psum | solution.py:158
  (122 shorter events, 22.6 us)
Async XLA Ops:
  7.2 6.0 %copy-start = (bf16[2048,512]{1,0:T(8,128)(2,1)S(1)}, bf16[2048,512]{1,0:T(8,128)(2,1)}, u32[]{:S(2)}) copy-start(bf16[2048,512]{1,0:T(8,128)(2,1)} %param.12) | copy-start | bytes 6291460
  7.2 33.9 %reduce-scatter.2.cloned.1.call-start = ((), (), s32[]{:S(2)}) async-start(), calls=%async_computation.5 | async-start | bytes 1310720 | tf_op jit(solution)/shard_map/reduce_scatter | solution.py:123
  8.1 7.8 %copy-start.34 = (s32[128]{0:T(128)S(1)}, s32[128]{0:T(128)}, u32[]{:S(2)}) copy-start(s32[128]{0:T(128)} %param.7) | copy-start | bytes 1540
  8.1 18.8 %collective-permute-start = (s32[3]{0:T(128)S(1)}, s32[3]{0:T(128)S(1)}, u32[]{:S(2)}, u32[]{:S(2)}) collective-permute-start(s32[3]{0:T(128)S(1)} %slice_add_fusion.2), channel_id=1, source_target_pairs={{0,4},{4,8},{8,12},{1,5},{5,9},{9,13},{2,6},{6,10},{10,14},{3,7},{... | collective-permute-start | bytes 44 | tf_op jit(solution)/shard_map/ppermute | solution.py:15
  15.9 8.8 %copy-start.17 = (f32[1,1,128,512]{3,2,1,0:T(8,128)S(1)}, f32[1,1,128,512]{3,2,1,0:T(8,128)}, u32[]{:S(2)}) copy-start(f32[1,1,128,512]{3,2,1,0:T(8,128)} %param.11) | copy-start | bytes 786436
  16.0 11.2 %copy-start.27 = (pred[128,5]{0,1:T(8,128)(4,1)}, pred[128,5]{0,1:T(8,128)(4,1)S(1)}, u32[]{:S(2)}) copy-start(pred[128,5]{0,1:T(8,128)(4,1)S(1)} %iota_compare_fusion.5) | copy-start | bytes 1924
  26.7 20.7 %copy-start.31 = (s32[128]{0:T(128)}, s32[128]{0:T(128)S(1)}, u32[]{:S(2)}) copy-start(s32[128]{0:T(128)S(1)} %broadcast_add_fusion) | copy-start | bytes 1540
  26.7 20.7 %copy-start.32 = (pred[128]{0:T(512)(128)(4,1)}, pred[128]{0:T(512)(128)(4,1)S(1)}, u32[]{:S(2)}) copy-start(pred[128]{0:T(512)(128)(4,1)S(1)} %compare_and_fusion) | copy-start | bytes 388
  26.7 20.7 %copy-start.33 = (s32[128]{0:T(128)}, s32[128]{0:T(128)S(1)}, u32[]{:S(2)}) copy-start(s32[128]{0:T(128)S(1)} %iota_and_fusion.1) | copy-start | bytes 1540
  26.8 55.6 %copy-start.24 = (pred[512]{0:T(512)(128)(4,1)}, pred[512]{0:T(512)(128)(4,1)S(1)}, u32[]{:S(2)}) copy-start(pred[512]{0:T(512)(128)(4,1)S(1)} %iota_compare_fusion.6) | copy-start | bytes 1540
  27.1 6.3 %copy-start.29 = (pred[128,5]{0,1:T(8,128)(4,1)}, pred[128,5]{0,1:T(8,128)(4,1)S(1)}, u32[]{:S(2)}) copy-start(pred[128,5]{0,1:T(8,128)(4,1)S(1)} %iota_compare_fusion.4) | copy-start | bytes 1924
  27.1 6.3 %copy-start.20 = (pred[128,5]{0,1:T(8,128)(4,1)}, pred[128,5]{0,1:T(8,128)(4,1)S(1)}, u32[]{:S(2)}) copy-start(pred[128,5]{0,1:T(8,128)(4,1)S(1)} %get-tuple-element.45) | copy-start | bytes 1924
  27.1 6.3 %copy-start.22 = (pred[128,5]{0,1:T(8,128)(4,1)}, pred[128,5]{0,1:T(8,128)(4,1)S(1)}, u32[]{:S(2)}) copy-start(pred[128,5]{0,1:T(8,128)(4,1)S(1)} %get-tuple-element.46) | copy-start | bytes 1924
  42.8 10.7 %all-to-all-start.2 = ((bf16[4,128,128]{1,2,0:T(8,128)(2,1)}), bf16[4,128,128]{1,2,0:T(8,128)(2,1)S(1)}, u32[]{:S(2)}, u32[]{:S(2)}) async-start(bf16[4,128,128]{1,2,0:T(8,128)(2,1)} %copy_bitcast_fusion), calls=%async_computation.3 | async-start | bytes 262144 | tf_op jit(solution)/shard_map/all_to_all | solution.py:133
  70.9 9.2 %all-to-all-start = ((bf16[4,128,128]{1,2,0:T(8,128)(2,1)}), bf16[4,128,128]{1,2,0:T(8,128)(2,1)S(1)}, u32[]{:S(2)}, u32[]{:S(2)}) async-start(bf16[4,128,128]{1,2,0:T(8,128)(2,1)} %copy.23), calls=%async_computation | async-start | bytes 262144 | tf_op jit(solution)/shard_map/all_to_all | solution.py:106
  88.8 9.9 %all-to-all-start.1 = ((bf16[128,4,128]{0,2,1:T(8,128)(2,1)}), bf16[128,4,128]{0,2,1:T(8,128)(2,1)}, u32[]{:S(2)}, u32[]{:S(2)}) async-start(bf16[128,4,128]{0,2,1:T(8,128)(2,1)} %bitcast.103), calls=%async_computation.1 | async-start | bytes 262144 | tf_op jit(solution)/shard_map/all_to_all | solution.py:110
  92.7 50.4 %all-reduce.2.cloned.1.call-start = ((), (), s32[]{:S(2)}) async-start(), calls=%async_computation.6 | async-start | bytes 2097152 | tf_op jit(solution)/shard_map/psum | solution.py:145
  100.5 6.1 %copy-start.14 = (f32[128,512]{1,0:T(8,128)S(1)}, f32[128,512]{1,0:T(8,128)}, u32[]{:S(2)}) copy-start(f32[128,512]{1,0:T(8,128)} %get-tuple-element.30) | copy-start | bytes 786436
  110.2 32.9 %copy-start.26 = (f32[128]{0:T(128)S(1)}, f32[128]{0:T(128)}, u32[]{:S(2)}) copy-start(f32[128]{0:T(128)} %copy-done.25) | copy-start | bytes 1540
  121.3 23.4 %copy-start.15 = (bf16[128,512]{1,0:T(8,128)(2,1)S(1)}, bf16[128,512]{1,0:T(8,128)(2,1)}, u32[]{:S(2)}) copy-start(bf16[128,512]{1,0:T(8,128)(2,1)} %param.13) | copy-start | bytes 393220
  121.4 23.4 %copy-start.21 = (pred[128,5]{0,1:T(8,128)(4,1)S(1)}, pred[128,5]{0,1:T(8,128)(4,1)}, u32[]{:S(2)}) copy-start(pred[128,5]{0,1:T(8,128)(4,1)} %copy-done.20) | copy-start | bytes 1924
  121.4 23.4 %copy-start.23 = (pred[128,5]{0,1:T(8,128)(4,1)S(1)}, pred[128,5]{0,1:T(8,128)(4,1)}, u32[]{:S(2)}) copy-start(pred[128,5]{0,1:T(8,128)(4,1)} %copy-done.22) | copy-start | bytes 1924
  121.4 23.4 %copy-start.28 = (pred[128,5]{0,1:T(8,128)(4,1)S(1)}, pred[128,5]{0,1:T(8,128)(4,1)}, u32[]{:S(2)}) copy-start(pred[128,5]{0,1:T(8,128)(4,1)} %copy-done.27) | copy-start | bytes 1924
  121.4 23.4 %copy-start.30 = (pred[128,5]{0,1:T(8,128)(4,1)S(1)}, pred[128,5]{0,1:T(8,128)(4,1)}, u32[]{:S(2)}) copy-start(pred[128,5]{0,1:T(8,128)(4,1)} %copy-done.29) | copy-start | bytes 1924
  (17 other events, 34.1 us)
Sparse Core Ops, SparseCore 0:
  16.0 25.0 reduce-scatter.1
  106.7 36.3 all-reduce.1
where the time goes:
time: 175 us; the launch traced here: 174 us
  waiting for transfers between devices  42 us (24%)
  blocking collectives  37.7 us (22%)
  matrix products  27.1 us (15%)
  other arithmetic  26.3 us (15%)
  starting transfers between devices  17 us (10%)
  between operations  14.6 us (8%)
  local copies, waits for them, and re-layouts  8.85 us (5%)
    psum x1, waiting for transfers between devices, per_device(): lax.psum(jnp.einsum('dmc,mcr->dr', in_proj, d_proj, preferred_element_typ...  21.7 us
    psum x1, blocking collectives, per_device(): lax.psum(jnp.concatenate([table_part, gain_part[None, :]], axis=0), 'seq')  19.4 us
    all_gather x1, blocking collectives, per_device(): lax.all_gather(gated_rows, ('chan', 'pair'), axis=0, tiled=True)  10.1 us
    cos x1, other arithmetic, dft_matrix(): jnp.cos(idx.astype(jnp.float32) * (2.0 * math.pi / total))  8.74 us
    all_to_all x1, blocking collectives, per_device(): lax.all_to_all(d_mixed_cols, 'seq', split_axis=1, concat_axis=0, tiled=True)  8.31 us
    reduce_scatter x1, waiting for transfers between devices, per_device(): lax.psum_scatter(jnp.einsum('cd,rd->cr', weight_rows, cotangent, preferre...  7.66 us
    dot_general x3, matrix products, inverse_dft(): lax.dot_general(spec * weight, dft, (((1,), (1,)), ((), ())), precision=T...  6.62 us
    dot_general x1, matrix products, per_device(): jnp.einsum('dmc,mcr->dr', in_proj, d_proj, preferred_element_type=jnp.flo...  6.06 us
  transfers between devices with their start and end apart: 6, of which 5 were waited for; matrix products, arithmetic and copies ran while one was open for 17% of the time, Pallas kernels for 0%

commit v1 on v0

--- a/solution.py
+++ b/solution.py
@@ -7,6 +7,28 @@
 NORM_EPSILON = 1e-05
 PRECISE = lax.Precision.HIGHEST
 TRANSFORM_PRECISION = lax.Precision.HIGH
+
+
+def laid_out(pieces, dim):
+    pieces = jnp.moveaxis(pieces, 0, dim)
+    shape = pieces.shape
+    return pieces.reshape(*shape[:dim], shape[dim] * shape[dim + 1], *shape[dim + 2 :])
+
+
+def ring_gather(shard, axis, dim):
+    length = lax.axis_size(axis)
+    pairs = [(i, (i + 1) % length) for i in range(length)]
+    back = [(b, a) for a, b in pairs]
+    lower, upper = ([], [])
+    for lap in range(length - 1):
+        if lap % 2 == 0:
+            lower.append(lax.ppermute(lower[-1] if lower else shard, axis, pairs))
+        else:
+            upper.append(lax.ppermute(upper[-1] if upper else shard, axis, back))
+    blocks = jnp.stack([*lower[::-1], shard, *upper])
+    shift = lax.axis_index(axis) - len(lower)
+    blocks = blocks[(jnp.arange(length) - shift) % length]
+    return laid_out(blocks, dim)
 
 
 def from_behind(value, axis, steps):
@@ -112,7 +134,7 @@
     weight_rows = out_proj
     mixed_out = jnp.einsum(
         "cr,cd->rd",
-        lax.all_gather(gated_rows, ("chan", "pair"), axis=0, tiled=True),
+        ring_gather(gated_rows, ("chan", "pair"), 0),
         weight_rows,
         preferred_element_type=jnp.float32,
     )

time: 175 us -> 166 us (0.949)
  blocking collectives: 37.7 us -> 19.4 us
  waiting for transfers between devices: 42 us -> 35.5 us
  local copies, waits for them, and re-layouts: 8.85 us -> 15 us
  starting transfers between devices: 17 us -> 21.4 us
  other arithmetic: 26.3 us -> 29.2 us
  matrix products: 27.1 us -> 29.5 us
    all_gather x1 -> x0, blocking collectives: 10.1 us -> none  [per_device(): lax.all_gather(gated_rows, ('chan', 'pair'), axis=0, tiled=True)]
    all_to_all x1 -> x0, blocking collectives: 8.31 us -> none  [per_device(): lax.all_to_all(d_mixed_cols, 'seq', split_axis=1, concat_axis=0, tiled=True)]
    reduce_scatter x1, waiting for transfers between devices: 7.66 us -> 0.81 us  [per_device(): lax.psum_scatter(jnp.einsum('cd,rd->cr', weight_rows, cotangent, preferre...]
    gather x0 -> x2, local copies, waits for them, and re-layouts: none -> 4.61 us  [ring_gather(): blocks = blocks[(jnp.arange(length) - shift) % length]]
    all_to_all x0 -> x1, starting transfers between devices: none -> 3.94 us  [per_device(): lax.all_to_all(d_mixed_cols, 'seq', split_axis=1, concat_axis=0, tiled=True)]
    all_to_all x1, waiting for transfers between devices: 5.88 us -> 3.39 us  [per_device(): lax.all_to_all(mixed_in, 'seq', split_axis=0, concat_axis=1, tiled=True)]
    all_to_all x0 -> x1, waiting for transfers between devices: none -> 2.39 us  [per_device(): lax.all_to_all(d_mixed_cols, 'seq', split_axis=1, concat_axis=0, tiled=True)]
    another operation x1 -> x2, other arithmetic: 1.84 us -> 3.78 us
  transfers between devices with their start and end apart: 6 -> 10, of which waited for: 5 -> 7; matrix products, arithmetic and copies ran while one was open for 17% -> 35% of each run, Pallas kernels for 0% -> 0%
where the time goes in v1:
time: 166 us; the launch traced here: 165 us
  waiting for transfers between devices  35.5 us (21%)
  matrix products  29.5 us (18%)
  other arithmetic  29.2 us (18%)
  starting transfers between devices  21.4 us (13%)
  blocking collectives  19.4 us (12%)
  local copies, waits for them, and re-layouts  15 us (9%)
  between operations  14.6 us (9%)
    psum x1, waiting for transfers between devices, per_device(): lax.psum(jnp.einsum('dmc,mcr->dr', in_proj, d_proj, preferred_element_typ...  22.2 us
    psum x1, blocking collectives, per_device(): lax.psum(jnp.concatenate([table_part, gain_part[None, :]], axis=0), 'seq')  19.4 us
    cos x1, other arithmetic, dft_matrix(): jnp.cos(idx.astype(jnp.float32) * (2.0 * math.pi / total))  8.74 us
    dot_general x3, matrix products, inverse_dft(): lax.dot_general(spec * weight, dft, (((1,), (1,)), ((), ())), precision=T...  7.69 us
    dot_general x1, matrix products, per_device(): jnp.einsum('dmc,mcr->dr', in_proj, d_proj, preferred_element_type=jnp.flo...  5.96 us
    dot_general x3, matrix products, forward_dft(): jnp.dot(signal.astype(jnp.float32), dft, precision=TRANSFORM_PRECISION)  5.89 us
    ppermute x1, starting transfers between devices, from_behind(): lax.ppermute(value, axis, [(source, source + steps) for source in range(f...  5.08 us
    gather x2, local copies, waits for them, and re-layouts, ring_gather(): blocks = blocks[(jnp.arange(length) - shift) % length]  4.61 us
  transfers between devices with their start and end apart: 10, of which 7 were waited for; matrix products, arithmetic and copies ran while one was open for 35% of the time, Pallas kernels for 0%

profile of v1, /device:TPU:0, one launch (start us, length us, event | category | flops | bytes accessed | tf_op | source)
XLA Modules:
  0.0 164.6 jit_solution(14616138824947884174)
XLA Ops:
  8.1 5.1 %collective-permute-start = (s32[3]{0:T(128)S(1)}, s32[3]{0:T(128)S(1)}, u32[]{:S(2)}, u32[]{:S(2)}) collective-permute-start(s32[3]{0:T(128)S(1)} %slice_add_fusion.2), channel_id=1, source_target_pairs={{0,4},{4,8},{8,12},{1,5},{5,9},{9,13},{2,6},{6,10},{10,14},{3,7},{... | collective-permute-start | bytes 44 | tf_op jit(solution)/shard_map/ppermute | solution.py:37
  13.2 2.7 %fusion.69 = f32[2048,128]{0,1:T(8,128)} fusion(bf16[2048,512]{1,0:T(8,128)(2,1)S(1)} %copy-done, bf16[128,512]{1,0:T(8,128)(2,1)} %param.13), kind=kOutput, calls=%fused_computation.155 | convolution fusion | flops 268435456 | bytes 3276800 | tf_op jit(solution)/shard_map/cd,rd->cr/dot_general | solution.py:146
  16.0 8.7 %fusion.5 = f32[512,1024]{1,0:T(8,128)S(1)} fusion(s32[1024]{0:T(1024)S(1)} %fusion.51, s32[512]{0:T(512)S(1)} %bitcast.118, pred[1024]{0:T(1024)(128)(4,1)S(1)} %iota_compare_fusion.1), kind=kLoop, calls=%fused_computation.16 | loop fusion | flops 15728640 | bytes 2104320 | tf_op jit(solution)/shard_map/cos | solution.py:49
  27.3 2.0 %maximum_select_fusion = f32[128,1024]{1,0:T(8,128)} fusion(f32[1,1024]{1,0:T(1,128)S(1)} %get-tuple-element.36, f32[127,1024]{1,0:T(8,128)} %get-tuple-element.38, f32[127,1024]{1,0:T(8,128)S(1)} %get-tuple-element.37, f32[1,1024]{1,0:T(1,128)S(1)} %get-tuple-element.35, s32[128]{0:T(128)S(1)} %iota_and_fusion.1, s32[128]{0:T(128)S(1)} %broadcast_add_fusion, ...), kind=kLoop, calls=%fused_computation.41 | loop fusion | flops 655360 | bytes 1574016 | tf_op jit(solution)/shard_map/jit(_where)/select_n | solution.py:89
  30.2 4.3 %convolution_bitcast_fusion.1 = f32[3,512,128]{1,2,0:T(8,128)S(1)} fusion(bf16[2048,3,512]{2,0,1:T(8,128)(2,1)} %param.10, f32[128,2048]{1,0:T(8,128)S(1)} %broadcast_multiply_fusion.1, f32[2048]{0:T(1024)S(1)} %copy-done.16), kind=kOutput, calls=%fused_computation.18 | convolution fusion | flops 805830656 | bytes 8134656 | tf_op jit(solution)/shard_map/dr,dmc->mcr/dot_general | solution.py:119
  36.4 3.9 %all-to-all-start = ((bf16[4,128,128]{1,2,0:T(8,128)(2,1)}), bf16[4,128,128]{1,2,0:T(8,128)(2,1)S(1)}, u32[]{:S(2)}, u32[]{:S(2)}) async-start(bf16[4,128,128]{1,2,0:T(8,128)(2,1)} %copy.24), calls=%async_computation | async-start | bytes 262144 | tf_op jit(solution)/shard_map/all_to_all | solution.py:128
  42.8 3.4 %all-to-all-done = bf16[4,128,128]{1,2,0:T(8,128)(2,1)S(1)} async-done(((bf16[4,128,128]{1,2,0:T(8,128)(2,1)}), bf16[4,128,128]{1,2,0:T(8,128)(2,1)S(1)}, u32[]{:S(2)}, u32[]{:S(2)}) %all-to-all-start) | async-done | bytes 131104 | tf_op jit(solution)/shard_map/all_to_all | solution.py:128
  46.2 3.3 %all-to-all-start.2 = ((bf16[4,128,128]{1,2,0:T(8,128)(2,1)}), bf16[4,128,128]{1,2,0:T(8,128)(2,1)S(1)}, u32[]{:S(2)}, u32[]{:S(2)}) async-start(bf16[4,128,128]{1,2,0:T(8,128)(2,1)} %copy_bitcast_fusion), calls=%async_computation.3 | async-start | bytes 262144 | tf_op jit(solution)/shard_map/all_to_all | solution.py:155
  49.5 2.9 %fusion.68 = f32[128,1024]{1,0:T(8,128)} fusion(bf16[128,512]{0,1:T(8,128)(2,1)S(1)} %bitcast.113, f32[512,1024]{1,0:T(8,128)} %copy-done.1), kind=kOutput, calls=%fused_computation.154 | convolution fusion | flops 402653184 | bytes 2752512 | tf_op jit(solution)/shard_map/dot_general | solution.py:53
  52.4 3.0 %all-to-all-done.2 = bf16[4,128,128]{1,2,0:T(8,128)(2,1)S(1)} async-done(((bf16[4,128,128]{1,2,0:T(8,128)(2,1)}), bf16[4,128,128]{1,2,0:T(8,128)(2,1)S(1)}, u32[]{:S(2)}, u32[]{:S(2)}) %all-to-all-start.2) | async-done | bytes 131104 | tf_op jit(solution)/shard_map/all_to_all | solution.py:155
  55.4 2.3 %fusion.70 = f32[128,1024]{1,0:T(8,128)S(1)} fusion(bf16[128,512]{0,1:T(8,128)(2,1)S(1)} %bitcast.114, f32[512,1024]{1,0:T(8,128)} %copy-done.1), kind=kOutput, calls=%fused_computation.156 | convolution fusion | flops 402653184 | bytes 2752512 | tf_op jit(solution)/shard_map/dot_general | solution.py:53
  62.4 2.9 %convolution_convert_fusion.1 = bf16[128,512]{1,0:T(8,128)(2,1)S(1)} fusion(f32[512,1024]{1,0:T(8,128)} %copy-done.1, f32[128,512]{1,0:T(8,128)} %get-tuple-element.29, f32[128,512]{1,0:T(8,128)} %get-tuple-element.30, f32[1024]{0:T(1024)S(1)} %fusion.55), kind=kOutput, calls=%fused_computation.24 | convolution fusion | flops 402980864 | bytes 2756608 | tf_op jit(solution)/shard_map/dot_general | solution.py:61
  66.1 3.3 %all-to-all-start.1 = ((bf16[128,4,128]{0,2,1:T(8,128)(2,1)}), bf16[128,4,128]{0,2,1:T(8,128)(2,1)S(1)}, u32[]{:S(2)}, u32[]{:S(2)}) async-start(bf16[128,4,128]{0,2,1:T(8,128)(2,1)} %bitcast.112), calls=%async_computation.1 | async-start | bytes 262144 | tf_op jit(solution)/shard_map/all_to_all | solution.py:132
  72.6 2.8 %all-to-all-done.1 = bf16[128,4,128]{0,2,1:T(8,128)(2,1)S(1)} async-done(((bf16[128,4,128]{0,2,1:T(8,128)(2,1)}), bf16[128,4,128]{0,2,1:T(8,128)(2,1)S(1)}, u32[]{:S(2)}, u32[]{:S(2)}) %all-to-all-start.1) | async-done | bytes 131104 | tf_op jit(solution)/shard_map/all_to_all | solution.py:132
  75.3 3.9 %all-to-all-start.3 = ((bf16[128,4,128]{0,2,1:T(8,128)(2,1)}), bf16[128,4,128]{0,2,1:T(8,128)(2,1)}, u32[]{:S(2)}, u32[]{:S(2)}) async-start(bf16[128,4,128]{0,2,1:T(8,128)(2,1)} %bitcast.111), calls=%async_computation.4 | async-start | bytes 262144 | tf_op jit(solution)/shard_map/all_to_all | solution.py:159
  82.9 2.4 %all-to-all-done.3 = bf16[128,4,128]{0,2,1:T(8,128)(2,1)} async-done(((bf16[128,4,128]{0,2,1:T(8,128)(2,1)}), bf16[128,4,128]{0,2,1:T(8,128)(2,1)}, u32[]{:S(2)}, u32[]{:S(2)}) %all-to-all-start.3) | async-done | bytes 131104 | tf_op jit(solution)/shard_map/all_to_all | solution.py:159
  90.7 2.0 %multiply_convert_fusion.1 = (bf16[1,512,128]{1,2,0:T(8,128)(2,1)S(1)}, bf16[1,512,128]{1,2,0:T(8,128)(2,1)S(1)}, bf16[1,512,128]{1,2,0:T(8,128)(2,1)}) fusion(f32[1,512,128]{1,2,0:T(8,128)} %reshape.182, f32[3,512,128]{1,2,0:T(8,128)} %copy-done.3, f32[1,512,128]{1,2,0:T(8,128)S(1)} %reshape.181), kind=kLoop, calls=%fused_computation.87 | loop fusion | flops 393216 | bytes 1703936 | tf_op jit(solution)/shard_map/convert.7
  92.7 6.0 %convolution_bitcast_fusion = f32[2048,128]{0,1:T(8,128)} fusion(bf16[2048,3,512]{2,0,1:T(8,128)(2,1)} %param.10, bf16[1,512,128]{1,2,0:T(8,128)(2,1)S(1)} %get-tuple-element.26, bf16[1,512,128]{1,2,0:T(8,128)(2,1)S(1)} %get-tuple-element.25, bf16[1,512,128]{1,2,0:T(8,128)(2,1)S(1)} %get-tuple-element.39), kind=kOutput, calls=%fused_computation.10 | convolution fusion | flops 805699584 | bytes 7733248 | tf_op jit(solution)/shard_map/dmc,mcr->dr/dot_general | solution.py:168
  98.8 3.6 %convolution_bitcast_fusion.3 = f32[1,1,128,512]{3,2,1,0:T(8,128)} fusion(f32[512,1024]{1,0:T(8,128)} %copy-done.1, f32[128,512]{1,0:T(8,128)} %get-tuple-element.32, f32[128,512]{1,0:T(8,128)S(1)} %copy-done.11, f32[1024]{0:T(1024)S(1)} %fusion.55), kind=kOutput, calls=%fused_computation.20 | convolution fusion | flops 402915328 | bytes 2887680 | tf_op jit(solution)/shard_map/dot_general | solution.py:61
  105.2 2.6 %gather_fusion = bf16[4,512,128]{1,2,0:T(8,128)(2,1)} fusion(bf16[4,512,128]{1,2,0:T(8,128)(2,1)} %pad_maximum_fusion.1, s32[1024]{0:T(1024)} %pad_clamp_fusion), kind=kCustom, calls=%fused_computation | custom fusion | bytes 1048592 | tf_op jit(solution)/shard_map/gather | solution.py:30
  107.8 2.0 %copy.28 = bf16[4,512,128]{2,1,0:T(8,128)(2,1)} copy(bf16[4,512,128]{1,2,0:T(8,128)(2,1)} %gather_fusion) | data formatting | bytes 1048576 | tf_op jit(solution)/shard_map/gather | solution.py:30
  109.8 2.2 %fusion.7 = bf16[128,512]{1,0:T(8,128)(2,1)} fusion(bf16[2048,128]{1,0:T(8,128)(2,1)} %bitcast.110, bf16[2048,512]{1,0:T(8,128)(2,1)S(1)} %copy-done, f32[128,2048]{1,0:T(8,128)S(1)} %get-tuple-element.47, s32[]{:T(128)S(6)} %select_n.157), kind=kOutput, calls=%fused_computation.22 | convolution fusion | flops 268566528 | bytes 3014660 | tf_op jit(solution)/shard_map/cr,cd->rd/dot_general | solution.py:135
  112.0 22.2 %all-reduce.2.cloned.1.call-done = f32[2048,128]{0,1:T(8,128)} async-done(((f32[2048,128]{0,1:T(8,128)}), f32[2048,128]{0,1:T(8,128)}) %all-reduce.2.cloned.1.call-update) | async-done | bytes 1048592 | tf_op jit(solution)/shard_map/psum | solution.py:167
  137.2 19.4 %psum.15 = f32[21,512]{1,0:T(8,128)S(1)} all-reduce(f32[21,512]{1,0:T(8,128)S(1)} %pad_maximum_fusion.2), channel_id=1, replica_groups=mesh['groups'=2,'seq'=4,'chan'=2,'pair'=2] {'seq'}, use_global_device_ids=true, to_apply=%region_5.6 | all-reduce | flops 10752 | bytes 86016 | tf_op jit(solution)/shard_map/psum | solution.py:180
  (130 shorter events, 33.3 us)
Async XLA Ops:
  7.2 6.0 %copy-start = (bf16[2048,512]{1,0:T(8,128)(2,1)S(1)}, bf16[2048,512]{1,0:T(8,128)(2,1)}, u32[]{:S(2)}) copy-start(bf16[2048,512]{1,0:T(8,128)(2,1)} %param.12) | copy-start | bytes 6291460
  7.2 33.9 %reduce-scatter.2.cloned.1.call-start = ((), (), s32[]{:S(2)}) async-start(), calls=%async_computation.5 | async-start | bytes 1310720 | tf_op jit(solution)/shard_map/reduce_scatter | solution.py:145
  8.1 7.8 %copy-start.31 = (s32[128]{0:T(128)S(1)}, s32[128]{0:T(128)}, u32[]{:S(2)}) copy-start(s32[128]{0:T(128)} %param.7) | copy-start | bytes 1540
  8.1 21.2 %collective-permute-start = (s32[3]{0:T(128)S(1)}, s32[3]{0:T(128)S(1)}, u32[]{:S(2)}, u32[]{:S(2)}) collective-permute-start(s32[3]{0:T(128)S(1)} %slice_add_fusion.2), channel_id=1, source_target_pairs={{0,4},{4,8},{8,12},{1,5},{5,9},{9,13},{2,6},{6,10},{10,14},{3,7},{... | collective-permute-start | bytes 44 | tf_op jit(solution)/shard_map/ppermute | solution.py:37
  15.9 8.8 %copy-start.14 = (f32[1,1,128,512]{3,2,1,0:T(8,128)S(1)}, f32[1,1,128,512]{3,2,1,0:T(8,128)}, u32[]{:S(2)}) copy-start(f32[1,1,128,512]{3,2,1,0:T(8,128)} %param.11) | copy-start | bytes 786436
  15.9 13.6 %copy-start.24 = (pred[128,5]{0,1:T(8,128)(4,1)}, pred[128,5]{0,1:T(8,128)(4,1)S(1)}, u32[]{:S(2)}) copy-start(pred[128,5]{0,1:T(8,128)(4,1)S(1)} %iota_compare_fusion.5) | copy-start | bytes 1924
  26.5 31.3 %copy-start.23 = (pred[512]{0:T(512)(128)(4,1)}, pred[512]{0:T(512)(128)(4,1)S(1)}, u32[]{:S(2)}) copy-start(pred[512]{0:T(512)(128)(4,1)S(1)} %iota_compare_fusion.6) | copy-start | bytes 1540
  29.5 5.2 %copy-start.26 = (pred[128,5]{0,1:T(8,128)(4,1)}, pred[128,5]{0,1:T(8,128)(4,1)S(1)}, u32[]{:S(2)}) copy-start(pred[128,5]{0,1:T(8,128)(4,1)S(1)} %iota_compare_fusion.4) | copy-start | bytes 1924
  29.5 5.2 %copy-start.17 = (pred[128,5]{0,1:T(8,128)(4,1)}, pred[128,5]{0,1:T(8,128)(4,1)S(1)}, u32[]{:S(2)}) copy-start(pred[128,5]{0,1:T(8,128)(4,1)S(1)} %get-tuple-element.48) | copy-start | bytes 1924
  36.4 9.8 %all-to-all-start = ((bf16[4,128,128]{1,2,0:T(8,128)(2,1)}), bf16[4,128,128]{1,2,0:T(8,128)(2,1)S(1)}, u32[]{:S(2)}, u32[]{:S(2)}) async-start(bf16[4,128,128]{1,2,0:T(8,128)(2,1)} %copy.24), calls=%async_computation | async-start | bytes 262144 | tf_op jit(solution)/shard_map/all_to_all | solution.py:128
  46.2 9.2 %all-to-all-start.2 = ((bf16[4,128,128]{1,2,0:T(8,128)(2,1)}), bf16[4,128,128]{1,2,0:T(8,128)(2,1)S(1)}, u32[]{:S(2)}, u32[]{:S(2)}) async-start(bf16[4,128,128]{1,2,0:T(8,128)(2,1)} %copy_bitcast_fusion), calls=%async_computation.3 | async-start | bytes 262144 | tf_op jit(solution)/shard_map/all_to_all | solution.py:155
  66.1 9.2 %all-to-all-start.1 = ((bf16[128,4,128]{0,2,1:T(8,128)(2,1)}), bf16[128,4,128]{0,2,1:T(8,128)(2,1)S(1)}, u32[]{:S(2)}, u32[]{:S(2)}) async-start(bf16[128,4,128]{0,2,1:T(8,128)(2,1)} %bitcast.112), calls=%async_computation.1 | async-start | bytes 262144 | tf_op jit(solution)/shard_map/all_to_all | solution.py:132
  75.3 9.9 %all-to-all-start.3 = ((bf16[128,4,128]{0,2,1:T(8,128)(2,1)}), bf16[128,4,128]{0,2,1:T(8,128)(2,1)}, u32[]{:S(2)}, u32[]{:S(2)}) async-start(bf16[128,4,128]{0,2,1:T(8,128)(2,1)} %bitcast.111), calls=%async_computation.4 | async-start | bytes 262144 | tf_op jit(solution)/shard_map/all_to_all | solution.py:159
  79.3 54.9 %all-reduce.2.cloned.1.call-start = ((), (), s32[]{:S(2)}) async-start(), calls=%async_computation.6 | async-start | bytes 2097152 | tf_op jit(solution)/shard_map/psum | solution.py:167
  81.1 17.6 %collective-permute-start.1 = (bf16[512,128]{0,1:T(8,128)(2,1)}, bf16[512,128]{0,1:T(8,128)(2,1)}, u32[]{:S(2)}, u32[]{:S(2)}) collective-permute-start(bf16[512,128]{0,1:T(8,128)(2,1)} %get-tuple-element.40), channel_id=1, source_target_pairs={{0,1},{1,2},{2,3},{3,0},{4,5},{5,6},{6,7},{7,4},{8,9},{9,10},{10,1... | collective-permute-start | bytes 393224 | tf_op jit(solution)/shard_map/ppermute | solution.py:25
  81.1 21.2 %collective-permute-start.3 = (bf16[512,128]{0,1:T(8,128)(2,1)}, bf16[512,128]{0,1:T(8,128)(2,1)}, u32[]{:S(2)}, u32[]{:S(2)}) collective-permute-start(bf16[512,128]{0,1:T(8,128)(2,1)} %get-tuple-element.40), channel_id=1, source_target_pairs={{1,0},{2,1},{3,2},{0,3},{5,4},{6,5},{7,6},{4,7},{9,8},{10,9},{11,1... | collective-permute-start | bytes 393224 | tf_op jit(solution)/shard_map/ppermute | solution.py:27
  92.7 6.1 %copy-start.11 = (f32[128,512]{1,0:T(8,128)S(1)}, f32[128,512]{1,0:T(8,128)}, u32[]{:S(2)}) copy-start(f32[128,512]{1,0:T(8,128)} %get-tuple-element.31) | copy-start | bytes 786436
  98.7 4.7 %collective-permute-start.2 = (bf16[512,128]{0,1:T(8,128)(2,1)}, bf16[512,128]{0,1:T(8,128)(2,1)S(1)}, u32[]{:S(2)}, u32[]{:S(2)}) collective-permute-start(bf16[512,128]{0,1:T(8,128)(2,1)} %collective-permute-done.1), channel_id=1, source_target_pairs={{0,1},{1,2},{2,3},{3,0},{4,5},{5,6},{6,7},{7,4},{8,9},{9,10},{10,1... | collective-permute-start | bytes 393224 | tf_op jit(solution)/shard_map/ppermute | solution.py:25
  107.8 26.4 %copy-start.22 = (f32[128]{0:T(128)S(1)}, f32[128]{0:T(128)}, u32[]{:S(2)}) copy-start(f32[128]{0:T(128)} %copy-done.21) | copy-start | bytes 1540
  112.0 23.8 %copy-start.12 = (bf16[128,512]{1,0:T(8,128)(2,1)S(1)}, bf16[128,512]{1,0:T(8,128)(2,1)}, u32[]{:S(2)}) copy-start(bf16[128,512]{1,0:T(8,128)(2,1)} %param.13) | copy-start | bytes 393220
  112.0 23.8 %copy-start.18 = (pred[128,5]{0,1:T(8,128)(4,1)S(1)}, pred[128,5]{0,1:T(8,128)(4,1)}, u32[]{:S(2)}) copy-start(pred[128,5]{0,1:T(8,128)(4,1)} %copy-done.17) | copy-start | bytes 1924
  112.0 23.8 %copy-start.20 = (pred[128,5]{0,1:T(8,128)(4,1)S(1)}, pred[128,5]{0,1:T(8,128)(4,1)}, u32[]{:S(2)}) copy-start(pred[128,5]{0,1:T(8,128)(4,1)} %copy-done.19) | copy-start | bytes 1924
  112.0 23.8 %copy-start.25 = (pred[128,5]{0,1:T(8,128)(4,1)S(1)}, pred[128,5]{0,1:T(8,128)(4,1)}, u32[]{:S(2)}) copy-start(pred[128,5]{0,1:T(8,128)(4,1)} %copy-done.24) | copy-start | bytes 1924
  112.0 23.8 %copy-start.27 = (pred[128,5]{0,1:T(8,128)(4,1)S(1)}, pred[128,5]{0,1:T(8,128)(4,1)}, u32[]{:S(2)}) copy-start(pred[128,5]{0,1:T(8,128)(4,1)} %copy-done.26) | copy-start | bytes 1924
  (18 other events, 52.9 us)
Sparse Core Ops, SparseCore 0:
  16.0 25.0 reduce-scatter.1
  98.8 35.2 all-reduce.1
